TPU v7x, 256 devices: a whole 4x4x8 slice. The times are simulated.
256 devices in a mesh: kv: 8 (over y, z_lo), blk: 32 (over x, z_hi, core).
Axes of the slice: x: 4, y: 4, z: 8 (z_hi: 4, z_lo: 2; z = z_hi * 2 + z_lo), core: 2. Of those that a mesh axis runs over, the one named last changes fastest.
Arguments:
- suffix_query: bfloat16 [6144, 4096], P('blk', 'kv'), may hold values from -6 to 6
- suffix_key_value: bfloat16 [2, 6144, 2048], P(None, 'blk', 'kv'), may hold values from -6 to 6
- suffix_resid: bfloat16 [6144, 4608], P('blk', 'kv'), may hold values from -6 to 6
- decode_query_rows: bfloat16 [64, 4096], P('blk', 'kv'), may hold values from -6 to 6
- decode_key_value: bfloat16 [2, 64, 2048], P(None, 'blk', 'kv'), may hold values from -6 to 6
- decode_resid: bfloat16 [64, 4608], P('blk', 'kv'), may hold values from -6 to 6
- out_weight: bfloat16 [4096, 4608], P('kv'), may hold values from -1.125 to 1.125
- post_gain: float32 [4608], P('kv'), may hold values from 0.1 to 1.9
- prefix_page_store: bfloat16 [2, 96, 128, 2048], P(None, 'blk', None, 'kv'), may hold values from -6 to 6
- prefix_table: int32 [96], replicated, may hold values from 0 to 95, each once
- decode_page_store: bfloat16 [2, 512, 128, 2048], P(None, 'blk', None, 'kv'), may hold values from -6 to 6
- page_table: int32 [512], replicated, may hold values from 0 to 511, each once
- suffix_lengths: int32 [16], replicated, may hold values from 1 to 768, 6144 in all
- suffix_prefix: int32 [16], replicated, may hold values from 0 to 3
- decode_ages: int32 [64], replicated, may hold values from 1 to 1023, as said below
Outputs:
- suffix_hidden: bfloat16 [6144, 4608], P('blk', 'kv')
- decode_hidden: bfloat16 [64, 4608], P('blk', 'kv')
- new_cache: bfloat16 [2, 512, 128, 2048], P(None, 'blk', None, 'kv')
Inputs may be any that keep to these rules, and one draw needn't show every extreme that they name: `page_table`: every page of the decode pool is named once. `prefix_table`: every page of the prefix pool is named once. `suffix_lengths`: the lengths sum to 6144; one is exactly 768. `decode_ages`: some slot has age 1024 - 1.
All inputs are finite; a program needn't handle non-finite values.
Results may differ from a plain program's by a relative error of at most 0.024.
Values may be sent and summed in bfloat16 or wider, within the bound.
No kernel may reach another device: no remote copies, remote signals or barrier semaphores. Data moves between devices by JAX's collectives and lax.ppermute only.
A program may use at most 128 MiB of HBM per device.

v0:
```python
import math
import jax
import jax.numpy as jnp
from jax import lax
from jax.sharding import PartitionSpec as P

D = 4608
QUERY_HEADS = 32
HEAD_SIZE = 128
PAGE_TOKENS = 128
PREFIX_LENGTH = 3072
SLOT_CAPACITY = 1024
soft_cap = 50.0
norm_eps = 1e-06


def from_behind(block, axis, distance):
    devices = range(lax.axis_size(axis))
    route = [(i - distance, i) for i in devices if i - distance in devices]
    return lax.ppermute(block, axis, route)


def attend(query_rows, key_rows, value_rows, visible, q_scale):
    logits = (
        jnp.einsum("qhgd,khd->qhgk", query_rows, key_rows, preferred_element_type=jnp.float32)
        * q_scale
    )
    capped = soft_cap * jnp.tanh(logits / soft_cap)
    weights = jnp.where(visible[:, None, None, :], jnp.exp(capped), 0.0)
    denominator = jnp.sum(weights, axis=3)
    numerator = jnp.einsum(
        "qhgk,khd->qhgd",
        weights.astype(jnp.bfloat16),
        value_rows,
        preferred_element_type=jnp.float32,
    )
    return (numerator, denominator)


def earlier(block_rows):
    return from_behind(block_rows, "blk", 1)


def token_tables(lengths, prefix_ids, token_ids):
    suffix_ends = jnp.cumsum(lengths)
    starts = suffix_ends - lengths
    inside = (
        (token_ids[:, None] >= starts[None, :]) & (token_ids[:, None] < suffix_ends[None, :])
    ).astype(jnp.int32)
    tok_start = jnp.sum(inside * starts[None, :], axis=1)
    tok_prefix = jnp.sum(inside * prefix_ids[None, :], axis=1)
    return (tok_start, tok_prefix)


def inverse_rows(table, wanted):
    hits = (table[None, :] == wanted[:, None]).astype(jnp.int32)
    places = jnp.arange(table.shape[0], dtype=jnp.int32)
    return jnp.sum(hits * places[None, :], axis=1)


def body(
    suffix_query,
    suffix_key_value,
    suffix_resid,
    decode_query_rows,
    decode_key_value,
    decode_resid,
    out_weight,
    post_gain,
    prefix_page_store,
    prefix_table,
    decode_page_store,
    page_table,
    suffix_lengths,
    suffix_prefix,
    decode_ages,
):
    head_dim = HEAD_SIZE
    page_len = PAGE_TOKENS
    q_scale = (D // QUERY_HEADS) ** (-0.5)
    tok_rows = suffix_query.shape[0]
    q_heads = suffix_query.shape[1] // head_dim
    kv_heads = suffix_key_value.shape[2] // head_dim
    query_group_width = q_heads // kv_heads
    my_index = lax.axis_index("blk")
    own_queries = suffix_query.reshape(tok_rows, kv_heads, query_group_width, head_dim)
    token_ids = my_index * tok_rows + jnp.arange(tok_rows, dtype=jnp.int32)
    tok_start, tok_prefix = token_tables(suffix_lengths, suffix_prefix, token_ids)
    look_back = 4
    pieces_back = [suffix_key_value]
    for step in range(look_back):
        pieces_back.insert(0, earlier(pieces_back[0]))
    window = jnp.concatenate(pieces_back, axis=1)
    key_ids = (my_index - look_back) * tok_rows + jnp.arange(
        (look_back + 1) * tok_rows, dtype=jnp.int32
    )
    visible = (key_ids[None, :] >= tok_start[:, None]) & (key_ids[None, :] <= token_ids[:, None])
    window_keys = window[0].reshape((look_back + 1) * tok_rows, kv_heads, head_dim)
    window_values = window[1].reshape((look_back + 1) * tok_rows, kv_heads, head_dim)
    own_numer, own_denom = attend(own_queries, window_keys, window_values, visible, q_scale)
    pool_pages = prefix_table.shape[0]
    page_owner = inverse_rows(prefix_table, jnp.arange(pool_pages, dtype=jnp.int32)) // (
        PREFIX_LENGTH // PAGE_TOKENS
    )
    all_queries = lax.all_gather(suffix_query, "blk", axis=0, tiled=True)
    all_tokens = all_queries.shape[0]
    all_ids = jnp.arange(all_tokens, dtype=jnp.int32)
    unused_start, all_prefix = token_tables(suffix_lengths, suffix_prefix, all_ids)
    local_pages = prefix_page_store.shape[1]
    held_owner = lax.dynamic_slice_in_dim(page_owner, my_index * local_pages, local_pages, 0)
    held_cols = jnp.repeat(held_owner, page_len)
    held_keys = prefix_page_store[0].reshape(local_pages * page_len, kv_heads, head_dim)
    held_values = prefix_page_store[1].reshape(local_pages * page_len, kv_heads, head_dim)
    block_rows = math.gcd(all_tokens, 1024)
    query_blocks = all_queries.reshape(
        all_tokens // block_rows, block_rows, kv_heads, query_group_width, head_dim
    )
    prefix_blocks = all_prefix.reshape(all_tokens // block_rows, block_rows)

    def one_block(element):
        block_queries, block_prefix = element
        seen = block_prefix[:, None] == held_cols[None, :]
        return attend(block_queries, held_keys, held_values, seen, q_scale)

    numer_all, denom_all = lax.map(one_block, (query_blocks, prefix_blocks))
    numer_all = numer_all.reshape(all_tokens, kv_heads, query_group_width, head_dim)
    denom_all = denom_all.reshape(all_tokens, kv_heads, query_group_width)
    pre_numer, pre_denom = (
        lax.psum_scatter(
            numer_all.astype(jnp.bfloat16), "blk", scatter_dimension=0, tiled=True
        ).astype(jnp.float32),
        lax.psum_scatter(
            denom_all.astype(jnp.bfloat16), "blk", scatter_dimension=0, tiled=True
        ).astype(jnp.float32),
    )
    suffix_attn = ((own_numer + pre_numer) / (own_denom + pre_denom)[..., None]).astype(
        jnp.bfloat16
    )
    suffix_attn = suffix_attn.reshape(tok_rows, q_heads * head_dim)
    all_dq, all_dkv = (
        lax.all_gather(decode_query_rows, "blk", axis=0, tiled=True),
        lax.all_gather(decode_key_value, "blk", axis=1, tiled=True),
    )
    slot_total = all_dq.shape[0]
    slot_pages = SLOT_CAPACITY // PAGE_TOKENS
    local_cache = decode_page_store.shape[1]
    page_ids = my_index * local_cache + jnp.arange(local_cache, dtype=jnp.int32)
    position = inverse_rows(page_table, page_ids)
    slot_of = position // slot_pages
    block_of = position % slot_pages
    slot_hot = slot_of[:, None] == jnp.arange(slot_total, dtype=jnp.int32)[None, :]
    page_age = jnp.sum(slot_hot.astype(jnp.int32) * decode_ages[None, :], axis=1)
    select = slot_hot.astype(jnp.bfloat16)
    new_rows = jnp.einsum(
        "ls,tsc->tlc", select, all_dkv, preferred_element_type=jnp.float32
    ).astype(jnp.bfloat16)
    write_here = (block_of == page_age // page_len)[:, None] & (
        jnp.arange(page_len, dtype=jnp.int32)[None, :] == (page_age % page_len)[:, None]
    )
    new_cache = jnp.where(write_here[None, :, :, None], new_rows[:, :, None, :], decode_page_store)
    page_queries = jnp.dot(select, all_dq, preferred_element_type=jnp.float32).astype(jnp.bfloat16)
    page_queries = page_queries.reshape(local_cache, kv_heads, query_group_width, head_dim)
    key_cache = new_cache[0].reshape(local_cache, page_len, kv_heads, head_dim)
    value_cache = new_cache[1].reshape(local_cache, page_len, kv_heads, head_dim)
    logits = (
        jnp.einsum("lhgd,lphd->lhgp", page_queries, key_cache, preferred_element_type=jnp.float32)
        * q_scale
    )
    capped = soft_cap * jnp.tanh(logits / soft_cap)
    places = block_of[:, None] * page_len + jnp.arange(page_len, dtype=jnp.int32)[None, :]
    seen_pos = places <= page_age[:, None]
    weights = jnp.where(seen_pos[:, None, None, :], jnp.exp(capped), 0.0)
    page_denom = jnp.sum(weights, axis=3)
    page_numer = jnp.einsum(
        "lhgp,lphd->lhgd",
        weights.astype(jnp.bfloat16),
        value_cache,
        preferred_element_type=jnp.float32,
    )
    slot_float = slot_hot.astype(jnp.float32)
    slot_numer = jnp.einsum(
        "ls,lhgd->shgd", slot_float, page_numer, precision=lax.Precision.HIGHEST
    )
    slot_denom = jnp.einsum("ls,lhg->shg", slot_float, page_denom, precision=lax.Precision.HIGHEST)
    mine_numer, mine_denom = (
        lax.psum_scatter(
            slot_numer.astype(jnp.bfloat16), "blk", scatter_dimension=0, tiled=True
        ).astype(jnp.float32),
        lax.psum_scatter(
            slot_denom.astype(jnp.bfloat16), "blk", scatter_dimension=0, tiled=True
        ).astype(jnp.float32),
    )
    decode_attn = (mine_numer / mine_denom[..., None]).astype(jnp.bfloat16)
    decode_rows = decode_attn.shape[0]
    decode_attn = decode_attn.reshape(decode_rows, q_heads * head_dim)
    attention = jnp.concatenate([suffix_attn, decode_attn], axis=0)
    projected = jnp.dot(attention, out_weight, preferred_element_type=jnp.float32)
    residual = jnp.concatenate([suffix_resid, decode_resid], axis=0).astype(jnp.float32)
    mine = lax.psum_scatter(
        projected.astype(jnp.bfloat16), "kv", scatter_dimension=1, tiled=True
    ).astype(jnp.float32)
    mean_square = lax.psum(jnp.sum(mine * mine, axis=1), "kv") / D
    normed = mine * lax.rsqrt(mean_square + norm_eps)[:, None] * post_gain[None, :]
    hidden = (residual + normed).astype(jnp.bfloat16)
    return (hidden[:tok_rows], hidden[tok_rows:], new_cache)


def solution(mesh):
    placed = (
        P("blk", "kv"),
        P(None, "blk", "kv"),
        P("blk", "kv"),
        P("blk", "kv"),
        P(None, "blk", "kv"),
        P("blk", "kv"),
        P("kv", None),
        P("kv"),
        P(None, "blk", None, "kv"),
        P(),
        P(None, "blk", None, "kv"),
        P(),
        P(),
        P(),
        P(),
    )
    return jax.shard_map(
        body,
        mesh=mesh,
        in_specs=placed,
        out_specs=(P("blk", "kv"), P("blk", "kv"), P(None, "blk", None, "kv")),
        check_vma=False,
    )
```

profile of v0, /device:TPU:2, one launch (start us, length us, event | category | flops | bytes accessed | tf_op | source)
XLA Modules:
  0.0 656.7 jit_solution(15037850193555876869)
XLA Ops:
  8.7 3.9 copy.90
  12.6 42.1 %all-gather = bf16[32,2,512]{2,1,0:T(2,128)(2,1)S(1)} all-gather(bf16[1,2,512]{2,1,0:T(2,128)(2,1)S(1)} %bitcast.118), channel_id=1, replica_groups=mesh['kv'=8,'blk'=32] {'blk'}, dimensions={0}, use_global_device_ids=true | all-gather | bytes 67584 | tf_op jit(solution)/shard_map/all_gather | solution.py:141
  55.2 42.4 %all_gather.11 = bf16[2,64,256]{2,0,1:T(2,128)(2,1)S(1)} all-gather(bf16[2,2,256]{2,0,1:T(2,128)(2,1)S(1)} %copy.88), channel_id=1, replica_groups=mesh['kv'=8,'blk'=32] {'blk'}, dimensions={1}, use_global_device_ids=true | all-gather | bytes 67584 | tf_op jit(solution)/shard_map/all_gather | solution.py:142
  98.1 2.5 broadcast_select_fusion
  101.9 1.0 convolution_convert_fusion.1
  103.9 9.7 %reshape.292 = bf16[6,1024,2,2,128]{4,3,2,1,0:T(2,128)(2,1)} reshape(bf16[6144,512]{1,0:T(8,128)(2,1)} %all-gather.3.cloned.1.call-done) | data formatting | bytes 12582912 | tf_op jit(solution)/shard_map/reshape | solution.py:115
  113.6 49.5 %while.15 = (s32[]{:T(128)}, bf16[6,1024,2,2,128]{4,1,3,2,0:T(8,128)(2,1)}, bf16[6,1024,2,2]{1,3,2,0:T(2,128)(2,1)S(1)}, s32[6,1024]{1,0:T(8,128)S(1)}, bf16[6,1...) while((s32[]{:T(128)}, ...), condition=%wide.region_6.7_spmd.clone, body=%wide.region_4.6_spmd.clone.sunk | while | flops 818278400 | bytes 19439220 | solution.py:125
  114.0 2.0 constant_dynamic-slice_fusion.5
  115.9 2.7 bitcast_reduce_fusion.2
  118.6 3.2 bitcast_dynamic-update-slice_fusion.4
  122.2 2.0 constant_dynamic-slice_fusion.5
  124.2 2.7 bitcast_reduce_fusion.2
  126.9 3.2 bitcast_dynamic-update-slice_fusion.4
  130.5 2.0 constant_dynamic-slice_fusion.5
  132.4 2.7 bitcast_reduce_fusion.2
  135.1 3.2 bitcast_dynamic-update-slice_fusion.4
  138.7 2.0 constant_dynamic-slice_fusion.5
  140.6 2.7 bitcast_reduce_fusion.2
  143.3 3.2 bitcast_dynamic-update-slice_fusion.4
  146.9 2.0 constant_dynamic-slice_fusion.5
  148.9 2.7 bitcast_reduce_fusion.2
  151.6 3.2 bitcast_dynamic-update-slice_fusion.4
  155.2 2.0 constant_dynamic-slice_fusion.5
  157.1 2.7 bitcast_reduce_fusion.2
  159.8 3.2 bitcast_dynamic-update-slice_fusion.4
  163.1 5.8 copy.117
  168.9 6.3 reshape.304
  175.2 6.1 copy.85
  182.2 2.2 collective-permute-start
  186.0 125.5 %all-reduce.1 = bf16[64,2,2]{2,0,1:T(8,128)(2,1)S(1)} all-reduce(bf16[64,2,2]{2,0,1:T(8,128)(2,1)S(1)} %convolution_convert_fusion.2), channel_id=5, replica_groups=mesh['kv'=8,'blk'=32] {'blk'}, use_global_device_ids=true, to_apply=%region_14.15.clone | all-reduce | flops 256 | bytes 1024
  311.7 1.9 collective-permute-start.1
  313.7 8.1 %collective-permute-done.1 = bf16[2,192,256]{2,1,0:T(8,128)(2,1)S(1)} collective-permute-done((bf16[2,192,256]{2,1,0:T(8,128)(2,1)S(1)}, bf16[2,192,256]{2,1,0:T(8,128)(2,1)S(1)}, u32[]{:S(2)}, u32[]{:S(2)}) %collective-permute-start.1) | collective-permute-done | bytes 196640 | tf_op jit(solution)/shard_map/ppermute | solution.py:20
  321.8 1.9 collective-permute-start.2
  323.9 7.8 %collective-permute-done.2 = bf16[2,192,256]{2,1,0:T(8,128)(2,1)S(1)} collective-permute-done((bf16[2,192,256]{2,1,0:T(8,128)(2,1)S(1)}, bf16[2,192,256]{2,1,0:T(8,128)(2,1)S(1)}, u32[]{:S(2)}, u32[]{:S(2)}) %collective-permute-start.2) | collective-permute-done | bytes 196640 | tf_op jit(solution)/shard_map/ppermute | solution.py:20
  331.8 2.1 collective-permute-start.3
  333.9 9.5 %all-reduce.4.cloned.1.call-done = bf16[64,2,2,128]{3,0,2,1:T(8,128)(2,1)} async-done(((bf16[64,2,2,128]{3,0,2,1:T(8,128)(2,1)}), bf16[64,2,2,128]{3,0,2,1:T(8,128)(2,1)}) %all-reduce.4.cloned.1.call-update) | async-done | bytes 65552
  344.3 0.9 reshape_squeeze.19
  345.4 3.9 fusion.10
  349.2 99.7 %reduce-scatter.12.cloned.1.call-done = bf16[192,4]{1,0:T(8,128)(2,1)} async-done(((bf16[6144,4]{1,0:T(8,128)(2,1)}), bf16[192,4]{1,0:T(8,128)(2,1)}) %reduce-scatter.12.cloned.1.call-update) | async-done | bytes 1552
  448.9 0.9 reshape.305
  449.9 109.7 %reduce-scatter.10.cloned.1.call-done = bf16[192,2,2,128]{3,0,2,1:T(8,128)(2,1)} async-done(((bf16[6144,2,2,128]{3,0,2,1:T(8,128)(2,1)}), bf16[192,2,2,128]{3,0,2,1:T(8,128)(2,1)}) %reduce-scatter.10.cloned.1.call-update) | async-done | bytes 196624 | tf_op jit(solution)/shard_map/reduce_scatter | solution.py:129
  559.6 2.9 fusion.29
  562.8 4.7 convolution_convert_fusion
  567.5 4.0 copy.115
  571.6 2.6 copy.96
  574.2 56.4 %reduce-scatter.14.cloned.1.call-done = bf16[576,194]{1,0:T(8,128)(2,1)} async-done(((bf16[4608,194]{1,0:T(8,128)(2,1)}), bf16[576,194]{1,0:T(8,128)(2,1)}) %reduce-scatter.14.cloned.1.call-update) | async-done | bytes 223504
  630.5 1.1 copy.116
  631.8 16.9 %psum.7 = f32[194]{0:T(256)S(1)} all-reduce(f32[194]{0:T(256)S(1)} %fusion.32), channel_id=1, replica_groups=mesh['kv'=8,'blk'=32] {'kv'}, use_global_device_ids=true, to_apply=%region_17.18 | all-reduce | flops 194 | bytes 1552 | tf_op jit(solution)/shard_map/psum | solution.py:202
  (122 shorter events, 12.3 us)
Async XLA Ops:
  7.2 5.4 copy-start.6
  7.2 47.6 %copy-start.7 = (s32[512]{0:T(512)S(1)}, s32[512]{0:T(512)}, u32[]{:S(2)}) copy-start(s32[512]{0:T(512)} %param.28) | copy-start | bytes 6148
  7.2 90.3 %copy-start.10 = (s32[64]{0:T(128)S(1)}, s32[64]{0:T(128)}, u32[]{:S(2)}) copy-start(s32[64]{0:T(128)} %param.31) | copy-start | bytes 772
  7.2 96.7 %all-gather.3.cloned.1.call-start = ((), (), s32[]{:S(2)}) async-start(), calls=%async_computation.3 | async-start | bytes 6488064 | tf_op jit(solution)/shard_map/all_gather | solution.py:105
  7.9 335.4 %all-reduce.4.cloned.1.call-start = ((), (), s32[]{:S(2)}) async-start(), calls=%async_computation.7 | async-start | bytes 131072
  100.6 2.4 copy-start.11
  100.6 2.5 copy-start.8
  100.6 2.8 copy-start.9
  100.6 3.0 copy-start.1
  102.9 346.0 %reduce-scatter.12.cloned.1.call-start = ((), (), s32[]{:S(2)}) async-start(), calls=%async_computation.5 | async-start | bytes 1622016
  175.1 384.5 %reduce-scatter.10.cloned.1.call-start = ((), (), s32[]{:S(2)}) async-start(), calls=%async_computation.4 | async-start | bytes 6488064 | tf_op jit(solution)/shard_map/reduce_scatter | solution.py:129
  181.2 0.9 copy-start.3
  181.2 3.2 copy-start
  181.2 3.3 copy-start.12
  181.3 449.3 %reduce-scatter.14.cloned.1.call-start = ((), (), s32[]{:S(2)}) async-start(), calls=%async_computation.6 | async-start | bytes 2654208
  182.2 129.5 %collective-permute-start = (bf16[2,192,256]{2,1,0:T(8,128)(2,1)S(1)}, bf16[2,192,256]{2,1,0:T(8,128)(2,1)S(1)}, u32[]{:S(2)}, u32[]{:S(2)}) collective-permute-start(bf16[2,192,256]{2,1,0:T(8,128)(2,1)S(1)} %copy-done.3), channel_id=1, source_target_pairs={{0,1},{1,2},{2,3},{3,4},{4,5},{5,6},{6,7},{7,8},{8,9},{9,10},{10,1... | collective-permute-start | bytes 589832 | tf_op jit(solution)/shard_map/ppermute | solution.py:20
  311.7 10.1 %collective-permute-start.1 = (bf16[2,192,256]{2,1,0:T(8,128)(2,1)S(1)}, bf16[2,192,256]{2,1,0:T(8,128)(2,1)S(1)}, u32[]{:S(2)}, u32[]{:S(2)}) collective-permute-start(bf16[2,192,256]{2,1,0:T(8,128)(2,1)S(1)} %collective-permute-done), channel_id=1, source_target_pairs={{0,1},{1,2},{2,3},{3,4},{4,5},{5,6},{6,7},{7,8},{8,9},{9,10},{10,1... | collective-permute-start | bytes 589832 | tf_op jit(solution)/shard_map/ppermute | solution.py:20
  321.8 10.0 %collective-permute-start.2 = (bf16[2,192,256]{2,1,0:T(8,128)(2,1)S(1)}, bf16[2,192,256]{2,1,0:T(8,128)(2,1)S(1)}, u32[]{:S(2)}, u32[]{:S(2)}) collective-permute-start(bf16[2,192,256]{2,1,0:T(8,128)(2,1)S(1)} %collective-permute-done.1), channel_id=1, source_target_pairs={{0,1},{1,2},{2,3},{3,4},{4,5},{5,6},{6,7},{7,8},{8,9},{9,10},{10,1... | collective-permute-start | bytes 589832 | tf_op jit(solution)/shard_map/ppermute | solution.py:20
  331.8 12.4 %collective-permute-start.3 = (bf16[2,192,256]{2,1,0:T(8,128)(2,1)S(1)}, bf16[2,192,256]{2,1,0:T(8,128)(2,1)S(1)}, u32[]{:S(2)}, u32[]{:S(2)}) collective-permute-start(bf16[2,192,256]{2,1,0:T(8,128)(2,1)S(1)} %collective-permute-done.2), channel_id=1, source_target_pairs={{0,1},{1,2},{2,3},{3,4},{4,5},{5,6},{6,7},{7,8},{8,9},{9,10},{10,1... | collective-permute-start | bytes 589832 | tf_op jit(solution)/shard_map/ppermute | solution.py:20
  571.5 77.2 %copy-start.2 = (bf16[192,576]{1,0:T(8,128)(2,1)S(1)}, bf16[192,576]{1,0:T(8,128)(2,1)}, u32[]{:S(2)}) copy-start(bf16[192,576]{1,0:T(8,128)(2,1)} %param.19) | copy-start | bytes 663556
  571.5 77.2 %copy-start.4 = (f32[576]{0:T(1024)S(1)}, f32[576]{0:T(1024)}, u32[]{:S(2)}) copy-start(f32[576]{0:T(1024)} %param.24) | copy-start | bytes 6916
  571.6 77.2 %copy-start.5 = (bf16[2,576]{1,0:T(2,128)(2,1)S(1)}, bf16[2,576]{1,0:T(2,128)(2,1)}, u32[]{:S(2)}) copy-start(bf16[2,576]{1,0:T(2,128)(2,1)} %param.22) | copy-start | bytes 6916
Sparse Core Ops, SparseCore 0:
  10.5 72.2 all-gather.2
  103.0 240.3 all-reduce.3
  347.8 101.0 reduce-scatter.11
  452.8 106.7 reduce-scatter.9
  571.7 58.8 reduce-scatter.13
where the time goes:
time: 658 us; the launch traced here: 657 us
  waiting for transfers between devices  292 us (44%)
  blocking collectives  227 us (34%)
  local copies, waits for them, and re-layouts  58.4 us (9%)
  matrix products  49.5 us (8%)
  between operations  14.8 us (2%)
  starting transfers between devices  8.36 us (1%)
  other arithmetic  6.68 us (1%)
    unnamed x8, waiting for transfers between devices  166 us
    unnamed x1, blocking collectives  126 us
    reduce_scatter x1, waiting for transfers between devices, body(): lax.psum_scatter(numer_all.astype(jnp.bfloat16), 'blk', scatter_dimension...  110 us
    all_gather x1, blocking collectives, body(): lax.all_gather(decode_key_value, 'blk', axis=1, tiled=True)  42.4 us
    all_gather x1, blocking collectives, body(): lax.all_gather(decode_query_rows, 'blk', axis=0, tiled=True)  42.1 us
    unnamed x43, local copies, waits for them, and re-layouts  27.1 us
    dot_general x7, matrix products, attend(): jnp.einsum('qhgk,khd->qhgd', weights.astype(jnp.bfloat16), value_rows, pr...  22.1 us
    dot_general x7, matrix products, attend(): jnp.einsum('qhgd,khd->qhgk', query_rows, key_rows, preferred_element_type...  19.9 us
  transfers between devices with their start and end apart: 9, of which 6 were waited for; matrix products, arithmetic and copies ran while one was open for 15% of the time, Pallas kernels for 0%

commit v1 on v0

--- a/solution.py
+++ b/solution.py
@@ -138,7 +138,12 @@
     )
     suffix_attn = suffix_attn.reshape(tok_rows, q_heads * head_dim)
     all_dq, all_dkv = (
-        lax.all_gather(decode_query_rows, "blk", axis=0, tiled=True),
+        jnp.concatenate(
+            lax.all_to_all(
+                jnp.stack([decode_query_rows for _ in range(lax.axis_size("blk"))]), "blk", 0, 0
+            ),
+            axis=0,
+        ),
         lax.all_gather(decode_key_value, "blk", axis=1, tiled=True),
     )
     slot_total = all_dq.shape[0]

time: 658 us -> 636 us (0.967)
  blocking collectives: 227 us -> 184 us
  starting transfers between devices: 8.36 us -> 19.9 us
    all_gather x1 -> x0, blocking collectives: 42.1 us -> none  [body(): lax.all_gather(decode_query_rows, 'blk', axis=0, tiled=True)]
    all_to_all x0 -> x1, starting transfers between devices: none -> 11.6 us  [body(): lax.all_to_all(jnp.stack([decode_query_rows for _ in range(lax.axis_size(...]
    unnamed x43 -> x52, local copies, waits for them, and re-layouts: 27.1 us -> 26.1 us
  transfers between devices with their start and end apart: 9 -> 10, of which waited for: 6 -> 7; matrix products, arithmetic and copies ran while one was open for 15% -> 17% of each run, Pallas kernels for 0% -> 0%
where the time goes in v1:
time: 636 us; the launch traced here: 635 us
  waiting for transfers between devices  294 us (46%)
  blocking collectives  184 us (29%)
  local copies, waits for them, and re-layouts  62.1 us (10%)
  matrix products  52 us (8%)
  starting transfers between devices  19.9 us (3%)
  between operations  14.9 us (2%)
  other arithmetic  8.56 us (1%)
    unnamed x8, waiting for transfers between devices  169 us
    unnamed x1, blocking collectives  124 us
    reduce_scatter x1, waiting for transfers between devices, body(): lax.psum_scatter(numer_all.astype(jnp.bfloat16), 'blk', scatter_dimension...  110 us
    all_gather x1, blocking collectives, body(): lax.all_gather(decode_key_value, 'blk', axis=1, tiled=True)  43.1 us
    unnamed x52, local copies, waits for them, and re-layouts  26.1 us
    dot_general x7, matrix products, attend(): jnp.einsum('qhgk,khd->qhgd', weights.astype(jnp.bfloat16), value_rows, pr...  22.1 us
    dot_general x7, matrix products, attend(): jnp.einsum('qhgd,khd->qhgk', query_rows, key_rows, preferred_element_type...  19.9 us
    psum x1, blocking collectives, body(): mean_square = lax.psum(jnp.sum(mine * mine, axis=1), 'kv') / D  16.9 us
  transfers between devices with their start and end apart: 10, of which 7 were waited for; matrix products, arithmetic and copies ran while one was open for 17% of the time, Pallas kernels for 0%

profile of v1, /device:TPU:2, one launch (start us, length us, event | category | flops | bytes accessed | tf_op | source)
XLA Modules:
  0.0 635.1 jit_solution(5643624599501562028)
XLA Ops:
  7.9 1.3 stack.2
  9.2 11.6 %all-to-all-start = ((bf16[32,2,512]{2,1,0:T(2,128)(2,1)}), bf16[32,2,512]{2,1,0:T(2,128)(2,1)S(1)}, u32[]{:S(2)}, u32[]{:S(2)}) async-start(bf16[32,2,512]{2,1,0:T(2,128)(2,1)} %stack.2), calls=%async_computation.1 | async-start | bytes 131072 | tf_op jit(solution)/shard_map/all_to_all | solution.py:142
  26.0 2.4 copy.90
  29.1 43.1 %all_gather.7 = bf16[2,64,256]{2,0,1:T(2,128)(2,1)S(1)} all-gather(bf16[2,2,256]{2,0,1:T(2,128)(2,1)S(1)} %copy.88), channel_id=1, replica_groups=mesh['kv'=8,'blk'=32] {'blk'}, dimensions={1}, use_global_device_ids=true | all-gather | bytes 67584 | tf_op jit(solution)/shard_map/all_gather | solution.py:147
  72.9 2.5 broadcast_select_fusion
  75.4 1.2 fusion.66
  78.1 1.7 fusion.69
  80.5 1.6 convolution_convert_fusion.1
  82.9 9.7 %reshape.297 = bf16[6,1024,2,2,128]{4,3,2,1,0:T(2,128)(2,1)} reshape(bf16[6144,512]{1,0:T(8,128)(2,1)} %all-gather.2.cloned.1.call-done) | data formatting | bytes 12582912 | tf_op jit(solution)/shard_map/reshape | solution.py:115
  92.6 49.4 %while.15 = (s32[]{:T(128)}, bf16[6,1024,2,2,128]{4,1,3,2,0:T(8,128)(2,1)}, bf16[6,1024,2,2]{1,3,2,0:T(2,128)(2,1)S(1)}, s32[6,1024]{1,0:T(8,128)S(1)}, bf16[6,1...) while((s32[]{:T(128)}, ...), condition=%wide.region_6.7_spmd.clone, body=%wide.region_4.6_spmd.clone.sunk | while | flops 818278400 | bytes 19439220 | solution.py:125
  93.0 2.0 constant_dynamic-slice_fusion.5
  94.9 2.7 bitcast_reduce_fusion.2
  97.6 3.2 bitcast_dynamic-update-slice_fusion.4
  101.2 2.0 constant_dynamic-slice_fusion.5
  103.2 2.7 bitcast_reduce_fusion.2
  105.9 3.2 bitcast_dynamic-update-slice_fusion.4
  109.5 2.0 constant_dynamic-slice_fusion.5
  111.4 2.7 bitcast_reduce_fusion.2
  114.1 3.3 bitcast_dynamic-update-slice_fusion.4
  117.8 2.0 constant_dynamic-slice_fusion.5
  119.7 2.7 bitcast_reduce_fusion.2
  122.4 3.2 bitcast_dynamic-update-slice_fusion.4
  126.0 2.0 constant_dynamic-slice_fusion.5
  127.9 2.7 bitcast_reduce_fusion.2
  130.6 3.2 bitcast_dynamic-update-slice_fusion.4
  134.2 2.0 constant_dynamic-slice_fusion.5
  136.2 2.7 bitcast_reduce_fusion.2
  138.8 3.2 bitcast_dynamic-update-slice_fusion.4
  142.0 5.8 copy.117
  147.8 6.3 reshape.308
  154.2 6.1 copy.85
  161.1 2.1 collective-permute-start
  164.8 7.2 %collective-permute-done = bf16[2,192,256]{2,1,0:T(8,128)(2,1)S(1)} collective-permute-done((bf16[2,192,256]{2,1,0:T(8,128)(2,1)S(1)}, bf16[2,192,256]{2,1,0:T(8,128)(2,1)S(1)}, u32[]{:S(2)}, u32[]{:S(2)}) %collective-permute-start) | collective-permute-done | bytes 196640 | tf_op jit(solution)/shard_map/ppermute | solution.py:20
  171.9 1.9 collective-permute-start.1
  174.1 7.9 %collective-permute-done.1 = bf16[2,192,256]{2,1,0:T(8,128)(2,1)S(1)} collective-permute-done((bf16[2,192,256]{2,1,0:T(8,128)(2,1)S(1)}, bf16[2,192,256]{2,1,0:T(8,128)(2,1)S(1)}, u32[]{:S(2)}, u32[]{:S(2)}) %collective-permute-start.1) | collective-permute-done | bytes 196640 | tf_op jit(solution)/shard_map/ppermute | solution.py:20
  182.0 1.9 collective-permute-start.2
  184.2 123.5 %all-reduce.1 = bf16[64,2,2]{2,0,1:T(8,128)(2,1)S(1)} all-reduce(bf16[64,2,2]{2,0,1:T(8,128)(2,1)S(1)} %convolution_convert_fusion.2), channel_id=5, replica_groups=mesh['kv'=8,'blk'=32] {'blk'}, use_global_device_ids=true, to_apply=%region_14.15.clone | all-reduce | flops 256 | bytes 1024
  307.9 2.1 collective-permute-start.3
  310.0 11.7 %all-reduce.4.cloned.1.call-done = bf16[64,2,2,128]{3,0,2,1:T(8,128)(2,1)} async-done(((bf16[64,2,2,128]{3,0,2,1:T(8,128)(2,1)}), bf16[64,2,2,128]{3,0,2,1:T(8,128)(2,1)}) %all-reduce.4.cloned.1.call-update) | async-done | bytes 65552
  323.7 3.9 fusion.10
  327.6 99.7 %reduce-scatter.12.cloned.1.call-done = bf16[192,4]{1,0:T(8,128)(2,1)} async-done(((bf16[6144,4]{1,0:T(8,128)(2,1)}), bf16[192,4]{1,0:T(8,128)(2,1)}) %reduce-scatter.12.cloned.1.call-update) | async-done | bytes 1552
  428.3 109.7 %reduce-scatter.10.cloned.1.call-done = bf16[192,2,2,128]{3,0,2,1:T(8,128)(2,1)} async-done(((bf16[6144,2,2,128]{3,0,2,1:T(8,128)(2,1)}), bf16[192,2,2,128]{3,0,2,1:T(8,128)(2,1)}) %reduce-scatter.10.cloned.1.call-update) | async-done | bytes 196624 | tf_op jit(solution)/shard_map/reduce_scatter | solution.py:129
  538.0 2.9 fusion.29
  541.2 4.7 convolution_convert_fusion
  545.9 4.0 copy.115
  549.9 2.6 copy.96
  552.5 56.4 %reduce-scatter.14.cloned.1.call-done = bf16[576,194]{1,0:T(8,128)(2,1)} async-done(((bf16[4608,194]{1,0:T(8,128)(2,1)}), bf16[576,194]{1,0:T(8,128)(2,1)}) %reduce-scatter.14.cloned.1.call-update) | async-done | bytes 223504
  610.2 16.9 %psum.7 = f32[194]{0:T(256)S(1)} all-reduce(f32[194]{0:T(256)S(1)} %fusion.32), channel_id=1, replica_groups=mesh['kv'=8,'blk'=32] {'kv'}, use_global_device_ids=true, to_apply=%region_17.18 | all-reduce | flops 194 | bytes 1552 | tf_op jit(solution)/shard_map/psum | solution.py:207
  (134 shorter events, 20.7 us)
Async XLA Ops:
  7.2 18.8 %copy-start = (bf16[2,16,128,256]{3,2,1,0:T(8,128)(2,1)S(1)}, bf16[2,16,128,256]{3,2,1,0:T(8,128)(2,1)}, u32[]{:S(2)}) copy-start(bf16[2,16,128,256]{3,2,1,0:T(8,128)(2,1)} %param.27) | copy-start | bytes 6291460
  7.2 75.7 %all-gather.2.cloned.1.call-start = ((), (), s32[]{:S(2)}) async-start(), calls=%async_computation.4 | async-start | bytes 6488064 | tf_op jit(solution)/shard_map/all_gather | solution.py:105
  9.2 68.0 %all-to-all-start = ((bf16[32,2,512]{2,1,0:T(2,128)(2,1)}), bf16[32,2,512]{2,1,0:T(2,128)(2,1)S(1)}, u32[]{:S(2)}, u32[]{:S(2)}) async-start(bf16[32,2,512]{2,1,0:T(2,128)(2,1)} %stack.2), calls=%async_computation.1 | async-start | bytes 131072 | tf_op jit(solution)/shard_map/all_to_all | solution.py:142
  20.9 300.8 %all-reduce.4.cloned.1.call-start = ((), (), s32[]{:S(2)}) async-start(), calls=%async_computation.8 | async-start | bytes 131072
  21.8 2.6 copy-start.6
  22.5 2.0 copy-start.11
  23.4 5.0 copy-start.15
  23.4 48.9 %copy-start.10 = (s32[512]{0:T(512)S(1)}, s32[512]{0:T(512)}, u32[]{:S(2)}) copy-start(s32[512]{0:T(512)} %param.28) | copy-start | bytes 6148
  23.4 49.1 %copy-start.16 = (s32[64]{0:T(128)S(1)}, s32[64]{0:T(128)}, u32[]{:S(2)}) copy-start(s32[64]{0:T(128)} %param.31) | copy-start | bytes 772
  72.4 4.1 copy-start.13
  82.1 10.5 %copy-start.4 = (bf16[384,2,128]{2,0,1:T(8,128)(2,1)S(1)}, bf16[384,2,128]{2,0,1:T(8,128)(2,1)}, u32[]{:S(2)}) copy-start(bf16[384,2,128]{2,0,1:T(8,128)(2,1)} %copy.84) | copy-start | bytes 589828
  82.1 10.5 %copy-start.5 = (s32[3]{0:T(128)S(1)}, s32[3]{0:T(128)}, u32[]{:S(2)}) copy-start(s32[3]{0:T(128)} %dynamic_slice.17) | copy-start | bytes 40
  82.2 345.1 %reduce-scatter.12.cloned.1.call-start = ((), (), s32[]{:S(2)}) async-start(), calls=%async_computation.6 | async-start | bytes 1622016
  154.1 383.8 %reduce-scatter.10.cloned.1.call-start = ((), (), s32[]{:S(2)}) async-start(), calls=%async_computation.5 | async-start | bytes 6488064 | tf_op jit(solution)/shard_map/reduce_scatter | solution.py:129
  160.2 0.9 copy-start.3
  160.2 3.1 copy-start.1
  160.2 3.2 copy-start.17
  160.2 4.4 copy-start.7
  160.2 4.4 copy-start.12
  160.2 23.7 %copy-start.14 = (s32[16]{0:T(128)S(1)}, s32[16]{0:T(128)}, u32[]{:S(2)}) copy-start(s32[16]{0:T(128)} %copy-done.13) | copy-start | bytes 196
  160.3 448.6 %reduce-scatter.14.cloned.1.call-start = ((), (), s32[]{:S(2)}) async-start(), calls=%async_computation.7 | async-start | bytes 2654208
  161.1 10.8 %collective-permute-start = (bf16[2,192,256]{2,1,0:T(8,128)(2,1)S(1)}, bf16[2,192,256]{2,1,0:T(8,128)(2,1)S(1)}, u32[]{:S(2)}, u32[]{:S(2)}) collective-permute-start(bf16[2,192,256]{2,1,0:T(8,128)(2,1)S(1)} %copy-done.3), channel_id=1, source_target_pairs={{0,1},{1,2},{2,3},{3,4},{4,5},{5,6},{6,7},{7,8},{8,9},{9,10},{10,1... | collective-permute-start | bytes 589832 | tf_op jit(solution)/shard_map/ppermute | solution.py:20
  171.9 10.1 %collective-permute-start.1 = (bf16[2,192,256]{2,1,0:T(8,128)(2,1)S(1)}, bf16[2,192,256]{2,1,0:T(8,128)(2,1)S(1)}, u32[]{:S(2)}, u32[]{:S(2)}) collective-permute-start(bf16[2,192,256]{2,1,0:T(8,128)(2,1)S(1)} %collective-permute-done), channel_id=1, source_target_pairs={{0,1},{1,2},{2,3},{3,4},{4,5},{5,6},{6,7},{7,8},{8,9},{9,10},{10,1... | collective-permute-start | bytes 589832 | tf_op jit(solution)/shard_map/ppermute | solution.py:20
  182.0 125.9 %collective-permute-start.2 = (bf16[2,192,256]{2,1,0:T(8,128)(2,1)S(1)}, bf16[2,192,256]{2,1,0:T(8,128)(2,1)S(1)}, u32[]{:S(2)}, u32[]{:S(2)}) collective-permute-start(bf16[2,192,256]{2,1,0:T(8,128)(2,1)S(1)} %collective-permute-done.1), channel_id=1, source_target_pairs={{0,1},{1,2},{2,3},{3,4},{4,5},{5,6},{6,7},{7,8},{8,9},{9,10},{10,1... | collective-permute-start | bytes 589832 | tf_op jit(solution)/shard_map/ppermute | solution.py:20
  307.9 14.6 %collective-permute-start.3 = (bf16[2,192,256]{2,1,0:T(8,128)(2,1)S(1)}, bf16[2,192,256]{2,1,0:T(8,128)(2,1)S(1)}, u32[]{:S(2)}, u32[]{:S(2)}) collective-permute-start(bf16[2,192,256]{2,1,0:T(8,128)(2,1)S(1)} %collective-permute-done.2), channel_id=1, source_target_pairs={{0,1},{1,2},{2,3},{3,4},{4,5},{5,6},{6,7},{7,8},{8,9},{9,10},{10,1... | collective-permute-start | bytes 589832 | tf_op jit(solution)/shard_map/ppermute | solution.py:20
  549.9 77.2 %copy-start.2 = (bf16[192,576]{1,0:T(8,128)(2,1)S(1)}, bf16[192,576]{1,0:T(8,128)(2,1)}, u32[]{:S(2)}) copy-start(bf16[192,576]{1,0:T(8,128)(2,1)} %param.19) | copy-start | bytes 663556
  549.9 77.2 %copy-start.8 = (f32[576]{0:T(1024)S(1)}, f32[576]{0:T(1024)}, u32[]{:S(2)}) copy-start(f32[576]{0:T(1024)} %param.24) | copy-start | bytes 6916
  549.9 77.2 %copy-start.9 = (bf16[2,576]{1,0:T(2,128)(2,1)S(1)}, bf16[2,576]{1,0:T(2,128)(2,1)}, u32[]{:S(2)}) copy-start(bf16[2,576]{1,0:T(2,128)(2,1)} %param.22) | copy-start | bytes 6916
Sparse Core Ops, SparseCore 0:
  10.5 72.3 all-gather.1
  85.5 236.1 all-reduce.3
  326.1 101.0 reduce-scatter.11
  431.2 106.7 reduce-scatter.9
  550.1 58.8 reduce-scatter.13
